TPU v7x, 256 devices: a whole 4x4x8 slice. The times are simulated.
256 devices in a mesh: blk: 64 (over y, x_lo, z), team: 4 (over x_hi, core).
Axes of the slice: x: 4 (x_hi: 2, x_lo: 2; x = x_hi * 2 + x_lo), y: 4, z: 8, core: 2. Of those that a mesh axis runs over, the one named last changes fastest.
Arguments:
- loadings: bfloat16 [64, 98304], P(None, ('blk', 'team')), may hold values from -6 to 6
- scales: bfloat16 [64, 768], P(None, ('blk', 'team')), may hold values from 0.25 to 4
- cov: bfloat16 [16384, 16, 4, 1536], P('blk', None, 'team'), may hold values from -0.01953125 to 0.01953125
Outputs:
- product: float32 [64, 16384], P(None, 'blk')
All inputs are finite; a program needn't handle non-finite values.
Results may differ from a plain program's by a relative error of at most 0.0028.
Values may be sent and summed in bfloat16 or wider, within the bound.
No kernel may reach another device: no remote copies, remote signals or barrier semaphores. Data moves between devices by JAX's collectives and lax.ppermute only.
A program may use at most 128 MiB of HBM per device.

v0:
```python
import jax
import jax.numpy as jnp
from jax import lax
from jax.sharding import PartitionSpec as P


def passed_along(x, axis, by):
    size = lax.axis_size(axis)
    return lax.ppermute(x, axis, [(i, (i + by) % size) for i in range(size)])


def per_device(loadings, scales, cov):
    team_size = lax.axis_size("team")
    cycle_size = lax.axis_size("blk")
    cycle_stops = cycle_size // team_size
    cycle_pos = lax.axis_index("blk")
    member = lax.axis_index("team")
    skew_lag = jnp.mod(cycle_pos - member, team_size)
    base_stop = jnp.mod((cycle_pos - skew_lag - member) // team_size, cycle_stops)
    held_block = (
        lax.all_gather(loadings, "team", axis=1, tiled=True),
        lax.all_gather(scales, "team", axis=1, tiled=True),
    )
    near_copy = passed_along((held_block[0], held_block[1]), "blk", 1)
    far_copies = passed_along((held_block[0], held_block[1], near_copy[0], near_copy[1]), "blk", 2)
    stacked_loads = jnp.stack([held_block[0], near_copy[0], far_copies[0], far_copies[2]])
    stacked_scales = jnp.stack([held_block[1], near_copy[1], far_copies[1], far_copies[3]])
    start_block = (
        lax.dynamic_index_in_dim(stacked_loads, skew_lag, 0, keepdims=False),
        lax.dynamic_index_in_dim(stacked_scales, skew_lag, 0, keepdims=False),
    )
    cov_local = cov[:, :, 0, :]
    n_loads = loadings.shape[0]
    row_count = cov.shape[0]

    def contribute(running, block, stop_num):
        block_load, block_scale = block
        groups = block_scale.shape[1]
        scaled = (
            (
                block_load.astype(jnp.float32).reshape(
                    n_loads, groups, block_load.shape[1] // groups
                )
                * block_scale.astype(jnp.float32)[:, :, None]
            )
            .reshape(n_loads, block_load.shape[1])
            .astype(jnp.bfloat16)
        )
        cov_slab = lax.dynamic_index_in_dim(
            cov_local, jnp.mod(stop_num, cycle_stops), 1, keepdims=False
        )
        term = lax.dot_general(
            scaled, cov_slab, (((1,), (1,)), ((), ())), preferred_element_type=jnp.float32
        )
        return running + term

    initial = jnp.zeros((n_loads, row_count), jnp.float32)
    running = contribute(initial, start_block, base_stop)

    def onward(stop_num, carry):
        partial_sum, moving = carry
        moving = passed_along((moving[0], moving[1]), "blk", team_size)
        return (contribute(partial_sum, moving, base_stop - stop_num), moving)

    running, _ = lax.fori_loop(1, cycle_stops, onward, (running, start_block))
    product = lax.psum(running, "team")
    return product


def solution(mesh):
    placed = (P(None, ("blk", "team")), P(None, ("blk", "team")), P("blk", None, "team", None))
    return jax.shard_map(
        per_device, mesh=mesh, in_specs=placed, out_specs=P(None, "blk"), check_vma=False
    )
```

profile of v0, /device:TPU:1, one launch (start us, length us, event | category | flops | bytes accessed | tf_op | source)
XLA Modules:
  0.0 371.3 jit_solution(5446585981449639470)
XLA Ops:
  6.5 10.4 %all_gather.6 = bf16[64,1536]{1,0:T(8,128)(2,1)S(1)} all-gather(bf16[64,384]{1,0:T(8,128)(2,1)} %param.5), channel_id=1, replica_groups=mesh['blk'=64,'team'=4] {'team'}, dimensions={1}, use_global_device_ids=true | all-gather | bytes 245760 | tf_op jit(solution)/shard_map/all_gather | solution.py:21
  16.9 2.9 collective-permute-start.3
  19.8 7.4 %all-gather = bf16[4,3,64]{2,1,0:T(4,128)(2,1)S(1)} all-gather(bf16[1,3,64]{2,1,0:T(4,128)(2,1)} %bitcast.55), channel_id=1, replica_groups=mesh['blk'=64,'team'=4] {'team'}, dimensions={0}, use_global_device_ids=true | all-gather | bytes 1920 | tf_op jit(solution)/shard_map/all_gather | solution.py:22
  27.2 2.9 collective-permute-start.5
  31.2 6.3 %collective-permute-done.5 = bf16[64,12]{0,1:T(8,128)(2,1)S(1)} collective-permute-done((bf16[64,12]{0,1:T(8,128)(2,1)S(1)}, bf16[64,12]{0,1:T(8,128)(2,1)S(1)}, u32[]{:S(2)}, u32[]{:S(2)}) %collective-permute-start.5) | collective-permute-done | bytes 1568 | tf_op jit(solution)/shard_map/ppermute | solution.py:9
  38.2 4.4 %constant_dynamic-slice_fusion = bf16[256,1,1,1536]{3,1,2,0:T(2,128)(2,1)S(1)} fusion(bf16[256,16,1,1536]{3,1,2,0:T(8,128)(2,1)} %param.7, s32[]{:T(128)S(6)} %select_n.61), kind=kLoop, calls=%fused_computation.27 | loop fusion | bytes 1572868 | tf_op jit(solution)/shard_map/jit(dynamic_index_in_dim)/dynamic_slice | solution.py:49
  42.7 13.0 %copy.27 = bf16[256,16,1,1536]{3,0,1,2:T(8,128)(2,1)} copy(bf16[256,16,1,1536]{3,1,2,0:T(8,128)(2,1)} %param.7) | data formatting | bytes 25165824 | tf_op args[2]
  56.8 219.6 %while.19 = (s32[]{:T(128)}, f32[64,256]{1,0:T(8,128)S(1)}, bf16[64,1536]{1,0:T(8,128)(2,1)S(1)}, bf16[64,12]{1,0:T(8,128)(2,1)S(1)}, s32[]{:T(128)}, /*index=5*...) while((s32[]{:T(128)}, f32[64,256]{1,0:T(8,128)S(1)}, ...), condition=%wide.region_1.2_spmd, body=%wide.region_0.1_spmd.sunk | while | flops 50642960 | bytes 3091284 | solution.py:65
  56.9 2.6 collective-permute-start.1
  59.4 3.8 %collective-permute-start = (bf16[64,12]{1,0:T(8,128)(2,1)S(1)}, bf16[64,12]{1,0:T(8,128)(2,1)S(1)}, u32[]{:S(2)}, u32[]{:S(2)}) collective-permute-start(bf16[64,12]{1,0:T(8,128)(2,1)S(1)} %get-tuple-element.235), channel_id=1, source_target_pairs={{0,16},{4,20},{8,24},{12,28},{16,32},{20,36},{24,40},{28,44},{32,4... | collective-permute-start | bytes 4616 | tf_op jit(solution)/shard_map/while/body/eval_jaxpr/ppermute | solution.py:9
  63.2 8.5 %collective-permute-done = bf16[64,12]{1,0:T(8,128)(2,1)S(1)} collective-permute-done((bf16[64,12]{1,0:T(8,128)(2,1)S(1)}, bf16[64,12]{1,0:T(8,128)(2,1)S(1)}, u32[]{:S(2)}, u32[]{:S(2)}) %collective-permute-start) | collective-permute-done | bytes 1568 | tf_op jit(solution)/shard_map/while/body/eval_jaxpr/ppermute | solution.py:9
  74.2 5.7 %collective-permute-start = (bf16[64,12]{1,0:T(8,128)(2,1)S(1)}, bf16[64,12]{1,0:T(8,128)(2,1)S(1)}, u32[]{:S(2)}, u32[]{:S(2)}) collective-permute-start(bf16[64,12]{1,0:T(8,128)(2,1)S(1)} %get-tuple-element.235), channel_id=1, source_target_pairs={{0,16},{4,20},{8,24},{12,28},{16,32},{20,36},{24,40},{28,44},{32,4... | collective-permute-start | bytes 4616 | tf_op jit(solution)/shard_map/while/body/eval_jaxpr/ppermute | solution.py:9
  79.9 11.1 %collective-permute-done = bf16[64,12]{1,0:T(8,128)(2,1)S(1)} collective-permute-done((bf16[64,12]{1,0:T(8,128)(2,1)S(1)}, bf16[64,12]{1,0:T(8,128)(2,1)S(1)}, u32[]{:S(2)}, u32[]{:S(2)}) %collective-permute-start) | collective-permute-done | bytes 1568 | tf_op jit(solution)/shard_map/while/body/eval_jaxpr/ppermute | solution.py:9
  94.8 10.4 %collective-permute-done = bf16[64,12]{1,0:T(8,128)(2,1)S(1)} collective-permute-done((bf16[64,12]{1,0:T(8,128)(2,1)S(1)}, bf16[64,12]{1,0:T(8,128)(2,1)S(1)}, u32[]{:S(2)}, u32[]{:S(2)}) %collective-permute-start) | collective-permute-done | bytes 1568 | tf_op jit(solution)/shard_map/while/body/eval_jaxpr/ppermute | solution.py:9
  107.0 3.6 collective-permute-start
  110.6 8.2 %collective-permute-done = bf16[64,12]{1,0:T(8,128)(2,1)S(1)} collective-permute-done((bf16[64,12]{1,0:T(8,128)(2,1)S(1)}, bf16[64,12]{1,0:T(8,128)(2,1)S(1)}, u32[]{:S(2)}, u32[]{:S(2)}) %collective-permute-start) | collective-permute-done | bytes 1568 | tf_op jit(solution)/shard_map/while/body/eval_jaxpr/ppermute | solution.py:9
  120.6 4.6 %collective-permute-start = (bf16[64,12]{1,0:T(8,128)(2,1)S(1)}, bf16[64,12]{1,0:T(8,128)(2,1)S(1)}, u32[]{:S(2)}, u32[]{:S(2)}) collective-permute-start(bf16[64,12]{1,0:T(8,128)(2,1)S(1)} %get-tuple-element.235), channel_id=1, source_target_pairs={{0,16},{4,20},{8,24},{12,28},{16,32},{20,36},{24,40},{28,44},{32,4... | collective-permute-start | bytes 4616 | tf_op jit(solution)/shard_map/while/body/eval_jaxpr/ppermute | solution.py:9
  125.2 7.1 %collective-permute-done = bf16[64,12]{1,0:T(8,128)(2,1)S(1)} collective-permute-done((bf16[64,12]{1,0:T(8,128)(2,1)S(1)}, bf16[64,12]{1,0:T(8,128)(2,1)S(1)}, u32[]{:S(2)}, u32[]{:S(2)}) %collective-permute-start) | collective-permute-done | bytes 1568 | tf_op jit(solution)/shard_map/while/body/eval_jaxpr/ppermute | solution.py:9
  134.1 5.4 %collective-permute-start = (bf16[64,12]{1,0:T(8,128)(2,1)S(1)}, bf16[64,12]{1,0:T(8,128)(2,1)S(1)}, u32[]{:S(2)}, u32[]{:S(2)}) collective-permute-start(bf16[64,12]{1,0:T(8,128)(2,1)S(1)} %get-tuple-element.235), channel_id=1, source_target_pairs={{0,16},{4,20},{8,24},{12,28},{16,32},{20,36},{24,40},{28,44},{32,4... | collective-permute-start | bytes 4616 | tf_op jit(solution)/shard_map/while/body/eval_jaxpr/ppermute | solution.py:9
  139.5 6.3 %collective-permute-done = bf16[64,12]{1,0:T(8,128)(2,1)S(1)} collective-permute-done((bf16[64,12]{1,0:T(8,128)(2,1)S(1)}, bf16[64,12]{1,0:T(8,128)(2,1)S(1)}, u32[]{:S(2)}, u32[]{:S(2)}) %collective-permute-start) | collective-permute-done | bytes 1568 | tf_op jit(solution)/shard_map/while/body/eval_jaxpr/ppermute | solution.py:9
  147.8 6.4 %collective-permute-start = (bf16[64,12]{1,0:T(8,128)(2,1)S(1)}, bf16[64,12]{1,0:T(8,128)(2,1)S(1)}, u32[]{:S(2)}, u32[]{:S(2)}) collective-permute-start(bf16[64,12]{1,0:T(8,128)(2,1)S(1)} %get-tuple-element.235), channel_id=1, source_target_pairs={{0,16},{4,20},{8,24},{12,28},{16,32},{20,36},{24,40},{28,44},{32,4... | collective-permute-start | bytes 4616 | tf_op jit(solution)/shard_map/while/body/eval_jaxpr/ppermute | solution.py:9
  154.2 5.0 %collective-permute-done = bf16[64,12]{1,0:T(8,128)(2,1)S(1)} collective-permute-done((bf16[64,12]{1,0:T(8,128)(2,1)S(1)}, bf16[64,12]{1,0:T(8,128)(2,1)S(1)}, u32[]{:S(2)}, u32[]{:S(2)}) %collective-permute-start) | collective-permute-done | bytes 1568 | tf_op jit(solution)/shard_map/while/body/eval_jaxpr/ppermute | solution.py:9
  162.6 3.0 collective-permute-start
  165.6 7.0 %collective-permute-done = bf16[64,12]{1,0:T(8,128)(2,1)S(1)} collective-permute-done((bf16[64,12]{1,0:T(8,128)(2,1)S(1)}, bf16[64,12]{1,0:T(8,128)(2,1)S(1)}, u32[]{:S(2)}, u32[]{:S(2)}) %collective-permute-start) | collective-permute-done | bytes 1568 | tf_op jit(solution)/shard_map/while/body/eval_jaxpr/ppermute | solution.py:9
  177.0 10.0 %collective-permute-done = bf16[64,12]{1,0:T(8,128)(2,1)S(1)} collective-permute-done((bf16[64,12]{1,0:T(8,128)(2,1)S(1)}, bf16[64,12]{1,0:T(8,128)(2,1)S(1)}, u32[]{:S(2)}, u32[]{:S(2)}) %collective-permute-start) | collective-permute-done | bytes 1568 | tf_op jit(solution)/shard_map/while/body/eval_jaxpr/ppermute | solution.py:9
  190.2 12.2 %collective-permute-done = bf16[64,12]{1,0:T(8,128)(2,1)S(1)} collective-permute-done((bf16[64,12]{1,0:T(8,128)(2,1)S(1)}, bf16[64,12]{1,0:T(8,128)(2,1)S(1)}, u32[]{:S(2)}, u32[]{:S(2)}) %collective-permute-start) | collective-permute-done | bytes 1568 | tf_op jit(solution)/shard_map/while/body/eval_jaxpr/ppermute | solution.py:9
  204.3 13.2 %collective-permute-done = bf16[64,12]{1,0:T(8,128)(2,1)S(1)} collective-permute-done((bf16[64,12]{1,0:T(8,128)(2,1)S(1)}, bf16[64,12]{1,0:T(8,128)(2,1)S(1)}, u32[]{:S(2)}, u32[]{:S(2)}) %collective-permute-start) | collective-permute-done | bytes 1568 | tf_op jit(solution)/shard_map/while/body/eval_jaxpr/ppermute | solution.py:9
  219.4 14.1 %collective-permute-done = bf16[64,12]{1,0:T(8,128)(2,1)S(1)} collective-permute-done((bf16[64,12]{1,0:T(8,128)(2,1)S(1)}, bf16[64,12]{1,0:T(8,128)(2,1)S(1)}, u32[]{:S(2)}, u32[]{:S(2)}) %collective-permute-start) | collective-permute-done | bytes 1568 | tf_op jit(solution)/shard_map/while/body/eval_jaxpr/ppermute | solution.py:9
  235.5 12.3 %collective-permute-done = bf16[64,12]{1,0:T(8,128)(2,1)S(1)} collective-permute-done((bf16[64,12]{1,0:T(8,128)(2,1)S(1)}, bf16[64,12]{1,0:T(8,128)(2,1)S(1)}, u32[]{:S(2)}, u32[]{:S(2)}) %collective-permute-start) | collective-permute-done | bytes 1568 | tf_op jit(solution)/shard_map/while/body/eval_jaxpr/ppermute | solution.py:9
  250.1 11.1 %collective-permute-done = bf16[64,12]{1,0:T(8,128)(2,1)S(1)} collective-permute-done((bf16[64,12]{1,0:T(8,128)(2,1)S(1)}, bf16[64,12]{1,0:T(8,128)(2,1)S(1)}, u32[]{:S(2)}, u32[]{:S(2)}) %collective-permute-start) | collective-permute-done | bytes 1568 | tf_op jit(solution)/shard_map/while/body/eval_jaxpr/ppermute | solution.py:9
  264.2 10.6 %collective-permute-done = bf16[64,12]{1,0:T(8,128)(2,1)S(1)} collective-permute-done((bf16[64,12]{1,0:T(8,128)(2,1)S(1)}, bf16[64,12]{1,0:T(8,128)(2,1)S(1)}, u32[]{:S(2)}, u32[]{:S(2)}) %collective-permute-start) | collective-permute-done | bytes 1568 | tf_op jit(solution)/shard_map/while/body/eval_jaxpr/ppermute | solution.py:9
  277.1 85.8 %all-reduce.2.cloned.1.call-done = f32[64,256]{1,0:T(8,128)} async-done(((f32[64,256]{1,0:T(8,128)}), f32[64,256]{1,0:T(8,128)}) %all-reduce.2.cloned.1.call-update) | async-done | bytes 65552 | tf_op jit(solution)/shard_map/psum | solution.py:66
  (119 shorter events, 42.0 us)
Async XLA Ops:
  6.5 356.4 %all-reduce.2.cloned.1.call-start = ((), (), s32[]{:S(2)}) async-start(), calls=%async_computation | async-start | bytes 131072 | tf_op jit(solution)/shard_map/psum | solution.py:66
  16.9 20.6 %collective-permute-start.2 = (bf16[64,1536]{1,0:T(8,128)(2,1)S(1)}, bf16[64,1536]{1,0:T(8,128)(2,1)S(1)}, u32[]{:S(2)}, u32[]{:S(2)}) collective-permute-start(bf16[64,1536]{1,0:T(8,128)(2,1)S(1)} %all_gather.6), channel_id=1, source_target_pairs={{0,4},{4,8},{8,12},{12,16},{16,20},{20,24},{24,28},{28,32},{32,36}... | collective-permute-start | bytes 589832 | tf_op jit(solution)/shard_map/ppermute | solution.py:9
  16.9 39.0 %collective-permute-start.3 = (bf16[64,1536]{1,0:T(8,128)(2,1)S(1)}, bf16[64,1536]{1,0:T(8,128)(2,1)S(1)}, u32[]{:S(2)}, u32[]{:S(2)}) collective-permute-start(bf16[64,1536]{1,0:T(8,128)(2,1)S(1)} %all_gather.6), channel_id=1, source_target_pairs={{0,8},{4,12},{8,16},{12,20},{16,24},{20,28},{24,32},{28,36},{32,40... | collective-permute-start | bytes 589832 | tf_op jit(solution)/shard_map/ppermute | solution.py:9
  30.0 25.6 %collective-permute-start.6 = (bf16[64,12]{0,1:T(8,128)(2,1)S(1)}, bf16[64,12]{0,1:T(8,128)(2,1)S(1)}, u32[]{:S(2)}, u32[]{:S(2)}) collective-permute-start(bf16[64,12]{0,1:T(8,128)(2,1)S(1)} %bitcast.50), channel_id=1, source_target_pairs={{0,8},{4,12},{8,16},{12,20},{16,24},{20,28},{24,32},{28,36},{32,40... | collective-permute-start | bytes 4616 | tf_op jit(solution)/shard_map/ppermute | solution.py:9
  37.6 18.1 %collective-permute-start.7 = (bf16[64,12]{0,1:T(8,128)(2,1)S(1)}, bf16[64,12]{0,1:T(8,128)(2,1)S(1)}, u32[]{:S(2)}, u32[]{:S(2)}) collective-permute-start(bf16[64,12]{0,1:T(8,128)(2,1)S(1)} %collective-permute-done.5), channel_id=1, source_target_pairs={{0,8},{4,12},{8,16},{12,20},{16,24},{20,28},{24,32},{28,36},{32,40... | collective-permute-start | bytes 4616 | tf_op jit(solution)/shard_map/ppermute | solution.py:9
  37.6 18.4 %collective-permute-start.4 = (bf16[64,1536]{1,0:T(8,128)(2,1)S(1)}, bf16[64,1536]{1,0:T(8,128)(2,1)S(1)}, u32[]{:S(2)}, u32[]{:S(2)}) collective-permute-start(bf16[64,1536]{1,0:T(8,128)(2,1)S(1)} %collective-permute-done.2), channel_id=1, source_target_pairs={{0,8},{4,12},{8,16},{12,20},{16,24},{20,28},{24,32},{28,36},{32,40... | collective-permute-start | bytes 589832 | tf_op jit(solution)/shard_map/ppermute | solution.py:9
  56.9 14.9 %collective-permute-start.1 = (bf16[64,1536]{1,0:T(8,128)(2,1)S(1)}, bf16[64,1536]{1,0:T(8,128)(2,1)S(1)}, u32[]{:S(2)}, u32[]{:S(2)}) collective-permute-start(bf16[64,1536]{1,0:T(8,128)(2,1)S(1)} %get-tuple-element.234), channel_id=1, source_target_pairs={{0,16},{4,20},{8,24},{12,28},{16,32},{20,36},{24,40},{28,44},{32,4... | collective-permute-start | bytes 589832 | tf_op jit(solution)/shard_map/while/body/eval_jaxpr/ppermute | solution.py:9
  59.4 12.3 %collective-permute-start = (bf16[64,12]{1,0:T(8,128)(2,1)S(1)}, bf16[64,12]{1,0:T(8,128)(2,1)S(1)}, u32[]{:S(2)}, u32[]{:S(2)}) collective-permute-start(bf16[64,12]{1,0:T(8,128)(2,1)S(1)} %get-tuple-element.235), channel_id=1, source_target_pairs={{0,16},{4,20},{8,24},{12,28},{16,32},{20,36},{24,40},{28,44},{32,4... | collective-permute-start | bytes 4616 | tf_op jit(solution)/shard_map/while/body/eval_jaxpr/ppermute | solution.py:9
  73.4 17.6 %collective-permute-start.1 = (bf16[64,1536]{1,0:T(8,128)(2,1)S(1)}, bf16[64,1536]{1,0:T(8,128)(2,1)S(1)}, u32[]{:S(2)}, u32[]{:S(2)}) collective-permute-start(bf16[64,1536]{1,0:T(8,128)(2,1)S(1)} %get-tuple-element.234), channel_id=1, source_target_pairs={{0,16},{4,20},{8,24},{12,28},{16,32},{20,36},{24,40},{28,44},{32,4... | collective-permute-start | bytes 589832 | tf_op jit(solution)/shard_map/while/body/eval_jaxpr/ppermute | solution.py:9
  74.2 16.8 %collective-permute-start = (bf16[64,12]{1,0:T(8,128)(2,1)S(1)}, bf16[64,12]{1,0:T(8,128)(2,1)S(1)}, u32[]{:S(2)}, u32[]{:S(2)}) collective-permute-start(bf16[64,12]{1,0:T(8,128)(2,1)S(1)} %get-tuple-element.235), channel_id=1, source_target_pairs={{0,16},{4,20},{8,24},{12,28},{16,32},{20,36},{24,40},{28,44},{32,4... | collective-permute-start | bytes 4616 | tf_op jit(solution)/shard_map/while/body/eval_jaxpr/ppermute | solution.py:9
  92.7 12.5 %collective-permute-start.1 = (bf16[64,1536]{1,0:T(8,128)(2,1)S(1)}, bf16[64,1536]{1,0:T(8,128)(2,1)S(1)}, u32[]{:S(2)}, u32[]{:S(2)}) collective-permute-start(bf16[64,1536]{1,0:T(8,128)(2,1)S(1)} %get-tuple-element.234), channel_id=1, source_target_pairs={{0,16},{4,20},{8,24},{12,28},{16,32},{20,36},{24,40},{28,44},{32,4... | collective-permute-start | bytes 589832 | tf_op jit(solution)/shard_map/while/body/eval_jaxpr/ppermute | solution.py:9
  92.8 12.4 %collective-permute-start = (bf16[64,12]{1,0:T(8,128)(2,1)S(1)}, bf16[64,12]{1,0:T(8,128)(2,1)S(1)}, u32[]{:S(2)}, u32[]{:S(2)}) collective-permute-start(bf16[64,12]{1,0:T(8,128)(2,1)S(1)} %get-tuple-element.235), channel_id=1, source_target_pairs={{0,16},{4,20},{8,24},{12,28},{16,32},{20,36},{24,40},{28,44},{32,4... | collective-permute-start | bytes 4616 | tf_op jit(solution)/shard_map/while/body/eval_jaxpr/ppermute | solution.py:9
  106.9 11.9 %collective-permute-start.1 = (bf16[64,1536]{1,0:T(8,128)(2,1)S(1)}, bf16[64,1536]{1,0:T(8,128)(2,1)S(1)}, u32[]{:S(2)}, u32[]{:S(2)}) collective-permute-start(bf16[64,1536]{1,0:T(8,128)(2,1)S(1)} %get-tuple-element.234), channel_id=1, source_target_pairs={{0,16},{4,20},{8,24},{12,28},{16,32},{20,36},{24,40},{28,44},{32,4... | collective-permute-start | bytes 589832 | tf_op jit(solution)/shard_map/while/body/eval_jaxpr/ppermute | solution.py:9
  107.0 11.8 %collective-permute-start = (bf16[64,12]{1,0:T(8,128)(2,1)S(1)}, bf16[64,12]{1,0:T(8,128)(2,1)S(1)}, u32[]{:S(2)}, u32[]{:S(2)}) collective-permute-start(bf16[64,12]{1,0:T(8,128)(2,1)S(1)} %get-tuple-element.235), channel_id=1, source_target_pairs={{0,16},{4,20},{8,24},{12,28},{16,32},{20,36},{24,40},{28,44},{32,4... | collective-permute-start | bytes 4616 | tf_op jit(solution)/shard_map/while/body/eval_jaxpr/ppermute | solution.py:9
  120.5 11.8 %collective-permute-start.1 = (bf16[64,1536]{1,0:T(8,128)(2,1)S(1)}, bf16[64,1536]{1,0:T(8,128)(2,1)S(1)}, u32[]{:S(2)}, u32[]{:S(2)}) collective-permute-start(bf16[64,1536]{1,0:T(8,128)(2,1)S(1)} %get-tuple-element.234), channel_id=1, source_target_pairs={{0,16},{4,20},{8,24},{12,28},{16,32},{20,36},{24,40},{28,44},{32,4... | collective-permute-start | bytes 589832 | tf_op jit(solution)/shard_map/while/body/eval_jaxpr/ppermute | solution.py:9
  120.6 11.7 %collective-permute-start = (bf16[64,12]{1,0:T(8,128)(2,1)S(1)}, bf16[64,12]{1,0:T(8,128)(2,1)S(1)}, u32[]{:S(2)}, u32[]{:S(2)}) collective-permute-start(bf16[64,12]{1,0:T(8,128)(2,1)S(1)} %get-tuple-element.235), channel_id=1, source_target_pairs={{0,16},{4,20},{8,24},{12,28},{16,32},{20,36},{24,40},{28,44},{32,4... | collective-permute-start | bytes 4616 | tf_op jit(solution)/shard_map/while/body/eval_jaxpr/ppermute | solution.py:9
  134.0 11.7 %collective-permute-start.1 = (bf16[64,1536]{1,0:T(8,128)(2,1)S(1)}, bf16[64,1536]{1,0:T(8,128)(2,1)S(1)}, u32[]{:S(2)}, u32[]{:S(2)}) collective-permute-start(bf16[64,1536]{1,0:T(8,128)(2,1)S(1)} %get-tuple-element.234), channel_id=1, source_target_pairs={{0,16},{4,20},{8,24},{12,28},{16,32},{20,36},{24,40},{28,44},{32,4... | collective-permute-start | bytes 589832 | tf_op jit(solution)/shard_map/while/body/eval_jaxpr/ppermute | solution.py:9
  147.5 11.7 %collective-permute-start.1 = (bf16[64,1536]{1,0:T(8,128)(2,1)S(1)}, bf16[64,1536]{1,0:T(8,128)(2,1)S(1)}, u32[]{:S(2)}, u32[]{:S(2)}) collective-permute-start(bf16[64,1536]{1,0:T(8,128)(2,1)S(1)} %get-tuple-element.234), channel_id=1, source_target_pairs={{0,16},{4,20},{8,24},{12,28},{16,32},{20,36},{24,40},{28,44},{32,4... | collective-permute-start | bytes 589832 | tf_op jit(solution)/shard_map/while/body/eval_jaxpr/ppermute | solution.py:9
  160.9 11.7 %collective-permute-start.1 = (bf16[64,1536]{1,0:T(8,128)(2,1)S(1)}, bf16[64,1536]{1,0:T(8,128)(2,1)S(1)}, u32[]{:S(2)}, u32[]{:S(2)}) collective-permute-start(bf16[64,1536]{1,0:T(8,128)(2,1)S(1)} %get-tuple-element.234), channel_id=1, source_target_pairs={{0,16},{4,20},{8,24},{12,28},{16,32},{20,36},{24,40},{28,44},{32,4... | collective-permute-start | bytes 589832 | tf_op jit(solution)/shard_map/while/body/eval_jaxpr/ppermute | solution.py:9
  174.3 12.6 %collective-permute-start.1 = (bf16[64,1536]{1,0:T(8,128)(2,1)S(1)}, bf16[64,1536]{1,0:T(8,128)(2,1)S(1)}, u32[]{:S(2)}, u32[]{:S(2)}) collective-permute-start(bf16[64,1536]{1,0:T(8,128)(2,1)S(1)} %get-tuple-element.234), channel_id=1, source_target_pairs={{0,16},{4,20},{8,24},{12,28},{16,32},{20,36},{24,40},{28,44},{32,4... | collective-permute-start | bytes 589832 | tf_op jit(solution)/shard_map/while/body/eval_jaxpr/ppermute | solution.py:9
  175.1 11.8 %collective-permute-start = (bf16[64,12]{1,0:T(8,128)(2,1)S(1)}, bf16[64,12]{1,0:T(8,128)(2,1)S(1)}, u32[]{:S(2)}, u32[]{:S(2)}) collective-permute-start(bf16[64,12]{1,0:T(8,128)(2,1)S(1)} %get-tuple-element.235), channel_id=1, source_target_pairs={{0,16},{4,20},{8,24},{12,28},{16,32},{20,36},{24,40},{28,44},{32,4... | collective-permute-start | bytes 4616 | tf_op jit(solution)/shard_map/while/body/eval_jaxpr/ppermute | solution.py:9
  188.6 13.7 %collective-permute-start.1 = (bf16[64,1536]{1,0:T(8,128)(2,1)S(1)}, bf16[64,1536]{1,0:T(8,128)(2,1)S(1)}, u32[]{:S(2)}, u32[]{:S(2)}) collective-permute-start(bf16[64,1536]{1,0:T(8,128)(2,1)S(1)} %get-tuple-element.234), channel_id=1, source_target_pairs={{0,16},{4,20},{8,24},{12,28},{16,32},{20,36},{24,40},{28,44},{32,4... | collective-permute-start | bytes 589832 | tf_op jit(solution)/shard_map/while/body/eval_jaxpr/ppermute | solution.py:9
  188.7 13.6 %collective-permute-start = (bf16[64,12]{1,0:T(8,128)(2,1)S(1)}, bf16[64,12]{1,0:T(8,128)(2,1)S(1)}, u32[]{:S(2)}, u32[]{:S(2)}) collective-permute-start(bf16[64,12]{1,0:T(8,128)(2,1)S(1)} %get-tuple-element.235), channel_id=1, source_target_pairs={{0,16},{4,20},{8,24},{12,28},{16,32},{20,36},{24,40},{28,44},{32,4... | collective-permute-start | bytes 4616 | tf_op jit(solution)/shard_map/while/body/eval_jaxpr/ppermute | solution.py:9
  204.1 13.4 %collective-permute-start.1 = (bf16[64,1536]{1,0:T(8,128)(2,1)S(1)}, bf16[64,1536]{1,0:T(8,128)(2,1)S(1)}, u32[]{:S(2)}, u32[]{:S(2)}) collective-permute-start(bf16[64,1536]{1,0:T(8,128)(2,1)S(1)} %get-tuple-element.234), channel_id=1, source_target_pairs={{0,16},{4,20},{8,24},{12,28},{16,32},{20,36},{24,40},{28,44},{32,4... | collective-permute-start | bytes 589832 | tf_op jit(solution)/shard_map/while/body/eval_jaxpr/ppermute | solution.py:9
  204.1 13.3 %collective-permute-start = (bf16[64,12]{1,0:T(8,128)(2,1)S(1)}, bf16[64,12]{1,0:T(8,128)(2,1)S(1)}, u32[]{:S(2)}, u32[]{:S(2)}) collective-permute-start(bf16[64,12]{1,0:T(8,128)(2,1)S(1)} %get-tuple-element.235), channel_id=1, source_target_pairs={{0,16},{4,20},{8,24},{12,28},{16,32},{20,36},{24,40},{28,44},{32,4... | collective-permute-start | bytes 4616 | tf_op jit(solution)/shard_map/while/body/eval_jaxpr/ppermute | solution.py:9
  219.2 14.4 %collective-permute-start.1 = (bf16[64,1536]{1,0:T(8,128)(2,1)S(1)}, bf16[64,1536]{1,0:T(8,128)(2,1)S(1)}, u32[]{:S(2)}, u32[]{:S(2)}) collective-permute-start(bf16[64,1536]{1,0:T(8,128)(2,1)S(1)} %get-tuple-element.234), channel_id=1, source_target_pairs={{0,16},{4,20},{8,24},{12,28},{16,32},{20,36},{24,40},{28,44},{32,4... | collective-permute-start | bytes 589832 | tf_op jit(solution)/shard_map/while/body/eval_jaxpr/ppermute | solution.py:9
  219.3 14.3 %collective-permute-start = (bf16[64,12]{1,0:T(8,128)(2,1)S(1)}, bf16[64,12]{1,0:T(8,128)(2,1)S(1)}, u32[]{:S(2)}, u32[]{:S(2)}) collective-permute-start(bf16[64,12]{1,0:T(8,128)(2,1)S(1)} %get-tuple-element.235), channel_id=1, source_target_pairs={{0,16},{4,20},{8,24},{12,28},{16,32},{20,36},{24,40},{28,44},{32,4... | collective-permute-start | bytes 4616 | tf_op jit(solution)/shard_map/while/body/eval_jaxpr/ppermute | solution.py:9
  235.3 12.5 %collective-permute-start.1 = (bf16[64,1536]{1,0:T(8,128)(2,1)S(1)}, bf16[64,1536]{1,0:T(8,128)(2,1)S(1)}, u32[]{:S(2)}, u32[]{:S(2)}) collective-permute-start(bf16[64,1536]{1,0:T(8,128)(2,1)S(1)} %get-tuple-element.234), channel_id=1, source_target_pairs={{0,16},{4,20},{8,24},{12,28},{16,32},{20,36},{24,40},{28,44},{32,4... | collective-permute-start | bytes 589832 | tf_op jit(solution)/shard_map/while/body/eval_jaxpr/ppermute | solution.py:9
  235.4 12.4 %collective-permute-start = (bf16[64,12]{1,0:T(8,128)(2,1)S(1)}, bf16[64,12]{1,0:T(8,128)(2,1)S(1)}, u32[]{:S(2)}, u32[]{:S(2)}) collective-permute-start(bf16[64,12]{1,0:T(8,128)(2,1)S(1)} %get-tuple-element.235), channel_id=1, source_target_pairs={{0,16},{4,20},{8,24},{12,28},{16,32},{20,36},{24,40},{28,44},{32,4... | collective-permute-start | bytes 4616 | tf_op jit(solution)/shard_map/while/body/eval_jaxpr/ppermute | solution.py:9
  249.5 11.8 %collective-permute-start.1 = (bf16[64,1536]{1,0:T(8,128)(2,1)S(1)}, bf16[64,1536]{1,0:T(8,128)(2,1)S(1)}, u32[]{:S(2)}, u32[]{:S(2)}) collective-permute-start(bf16[64,1536]{1,0:T(8,128)(2,1)S(1)} %get-tuple-element.234), channel_id=1, source_target_pairs={{0,16},{4,20},{8,24},{12,28},{16,32},{20,36},{24,40},{28,44},{32,4... | collective-permute-start | bytes 589832 | tf_op jit(solution)/shard_map/while/body/eval_jaxpr/ppermute | solution.py:9
  263.0 11.8 %collective-permute-start.1 = (bf16[64,1536]{1,0:T(8,128)(2,1)S(1)}, bf16[64,1536]{1,0:T(8,128)(2,1)S(1)}, u32[]{:S(2)}, u32[]{:S(2)}) collective-permute-start(bf16[64,1536]{1,0:T(8,128)(2,1)S(1)} %get-tuple-element.234), channel_id=1, source_target_pairs={{0,16},{4,20},{8,24},{12,28},{16,32},{20,36},{24,40},{28,44},{32,4... | collective-permute-start | bytes 589832 | tf_op jit(solution)/shard_map/while/body/eval_jaxpr/ppermute | solution.py:9
  263.0 11.7 %collective-permute-start = (bf16[64,12]{1,0:T(8,128)(2,1)S(1)}, bf16[64,12]{1,0:T(8,128)(2,1)S(1)}, u32[]{:S(2)}, u32[]{:S(2)}) collective-permute-start(bf16[64,12]{1,0:T(8,128)(2,1)S(1)} %get-tuple-element.235), channel_id=1, source_target_pairs={{0,16},{4,20},{8,24},{12,28},{16,32},{20,36},{24,40},{28,44},{32,4... | collective-permute-start | bytes 4616 | tf_op jit(solution)/shard_map/while/body/eval_jaxpr/ppermute | solution.py:9
  (6 other events, 55.7 us)
Sparse Core Ops, SparseCore 0:
  277.2 85.6 all-reduce.1
where the time goes:
time: 372 us; the launch traced here: 371 us
  waiting for transfers between devices  239 us (64%)
  starting transfers between devices  54.3 us (15%)
  local copies, waits for them, and re-layouts  23 us (6%)
  matrix products  22.6 us (6%)
  blocking collectives  17.7 us (5%)
  between operations  13.5 us (4%)
    ppermute x36, waiting for transfers between devices, passed_along(): return lax.ppermute(x, axis, [(i, (i + by) % size) for i in range(size)])  153 us
    psum x1, waiting for transfers between devices, per_device(): product = lax.psum(running, 'team')  85.8 us
    ppermute x36, starting transfers between devices, passed_along(): return lax.ppermute(x, axis, [(i, (i + by) % size) for i in range(size)])  54.3 us
    dot_general x16, matrix products, contribute(): lax.dot_general(scaled, cov_slab, (((1,), (1,)), ((), ())), preferred_ele...  22.6 us
    unnamed x5, local copies, waits for them, and re-layouts  15.1 us
    all_gather x1, blocking collectives, per_device(): lax.all_gather(loadings, 'team', axis=1, tiled=True)  10.4 us
  transfers between devices with their start and end apart: 37, of which 17 were waited for; matrix products, arithmetic and copies ran while one was open for 5% of the time, Pallas kernels for 0%

commit v1 on v0

--- a/solution.py
+++ b/solution.py
@@ -63,7 +63,7 @@
         return (contribute(partial_sum, moving, base_stop - stop_num), moving)
 
     running, _ = lax.fori_loop(1, cycle_stops, onward, (running, start_block))
-    product = lax.psum(running, "team")
+    product = jnp.sum(lax.all_gather(running, "team"), axis=0)
     return product
 
 

time: 372 us -> 317 us (0.85)
  waiting for transfers between devices: 239 us -> 153 us
  blocking collectives: 17.7 us -> 63.5 us
  between operations: 13.5 us -> 0.06 us
    psum x1 -> x0, waiting for transfers between devices: 85.8 us -> none  [per_device(): product = lax.psum(running, 'team')]
    all_gather x0 -> x1, blocking collectives: none -> 45.7 us  [per_device(): product = jnp.sum(lax.all_gather(running, 'team'), axis=0)]
    unnamed x5 -> x2, local copies, waits for them, and re-layouts: 15.1 us -> 13 us
  transfers between devices with their start and end apart: 37 -> 36, of which waited for: 17 -> 16; matrix products, arithmetic and copies ran while one was open for 5% -> 6% of each run, Pallas kernels for 0% -> 0%
where the time goes in v1:
time: 317 us; the launch traced here: 316 us
  waiting for transfers between devices  153 us (48%)
  blocking collectives  63.5 us (20%)
  starting transfers between devices  54.6 us (17%)
  matrix products  22.5 us (7%)
  local copies, waits for them, and re-layouts  20.9 us (7%)
    ppermute x36, waiting for transfers between devices, passed_along(): return lax.ppermute(x, axis, [(i, (i + by) % size) for i in range(size)])  153 us
    ppermute x36, starting transfers between devices, passed_along(): return lax.ppermute(x, axis, [(i, (i + by) % size) for i in range(size)])  54.6 us
    all_gather x1, blocking collectives, per_device(): product = jnp.sum(lax.all_gather(running, 'team'), axis=0)  45.7 us
    dot_general x16, matrix products, contribute(): lax.dot_general(scaled, cov_slab, (((1,), (1,)), ((), ())), preferred_ele...  22.5 us
    unnamed x2, local copies, waits for them, and re-layouts  13 us
    all_gather x1, blocking collectives, per_device(): lax.all_gather(loadings, 'team', axis=1, tiled=True)  10.4 us
    all_gather x1, blocking collectives, per_device(): lax.all_gather(scales, 'team', axis=1, tiled=True)  7.35 us
  transfers between devices with their start and end apart: 36, of which 16 were waited for; matrix products, arithmetic and copies ran while one was open for 6% of the time, Pallas kernels for 0%

profile of v1, /device:TPU:1, one launch (start us, length us, event | category | flops | bytes accessed | tf_op | source)
XLA Modules:
  0.0 316.3 jit_solution(6297362508874855521)
XLA Ops:
  0.0 10.4 %all_gather.12 = bf16[64,1536]{1,0:T(8,128)(2,1)S(1)} all-gather(bf16[64,384]{1,0:T(8,128)(2,1)} %param.5), channel_id=1, replica_groups=mesh['blk'=64,'team'=4] {'team'}, dimensions={1}, use_global_device_ids=true | all-gather | bytes 245760 | tf_op jit(solution)/shard_map/all_gather | solution.py:21
  10.4 2.9 collective-permute-start.3
  13.3 7.4 %all-gather.1 = bf16[4,3,64]{2,1,0:T(4,128)(2,1)S(1)} all-gather(bf16[1,3,64]{2,1,0:T(4,128)(2,1)} %bitcast.57), channel_id=1, replica_groups=mesh['blk'=64,'team'=4] {'team'}, dimensions={0}, use_global_device_ids=true | all-gather | bytes 1920 | tf_op jit(solution)/shard_map/all_gather | solution.py:22
  20.6 2.9 collective-permute-start.5
  24.7 6.3 %collective-permute-done.5 = bf16[64,12]{0,1:T(8,128)(2,1)S(1)} collective-permute-done((bf16[64,12]{0,1:T(8,128)(2,1)S(1)}, bf16[64,12]{0,1:T(8,128)(2,1)S(1)}, u32[]{:S(2)}, u32[]{:S(2)}) %collective-permute-start.5) | collective-permute-done | bytes 1568 | tf_op jit(solution)/shard_map/ppermute | solution.py:9
  31.7 4.4 %constant_dynamic-slice_fusion = bf16[256,1,1,1536]{3,1,2,0:T(2,128)(2,1)S(1)} fusion(bf16[256,16,1,1536]{3,1,2,0:T(8,128)(2,1)} %param.7, s32[]{:T(128)S(6)} %select_n.61), kind=kLoop, calls=%fused_computation.27 | loop fusion | bytes 1572868 | tf_op jit(solution)/shard_map/jit(dynamic_index_in_dim)/dynamic_slice | solution.py:49
  36.1 13.0 %copy.27 = bf16[256,16,1,1536]{3,0,1,2:T(8,128)(2,1)} copy(bf16[256,16,1,1536]{3,1,2,0:T(8,128)(2,1)} %param.7) | data formatting | bytes 25165824 | tf_op args[2]
  50.3 219.6 %while.19 = (s32[]{:T(128)}, f32[64,256]{1,0:T(8,128)S(1)}, bf16[64,1536]{1,0:T(8,128)(2,1)S(1)}, bf16[64,12]{1,0:T(8,128)(2,1)S(1)}, s32[]{:T(128)}, /*index=5*...) while((s32[]{:T(128)}, f32[64,256]{1,0:T(8,128)S(1)}, ...), condition=%wide.region_1.2_spmd, body=%wide.region_0.1_spmd.sunk | while | flops 50642960 | bytes 3091284 | solution.py:65
  50.3 2.6 collective-permute-start.1
  52.9 3.8 %collective-permute-start = (bf16[64,12]{1,0:T(8,128)(2,1)S(1)}, bf16[64,12]{1,0:T(8,128)(2,1)S(1)}, u32[]{:S(2)}, u32[]{:S(2)}) collective-permute-start(bf16[64,12]{1,0:T(8,128)(2,1)S(1)} %get-tuple-element.235), channel_id=1, source_target_pairs={{0,16},{4,20},{8,24},{12,28},{16,32},{20,36},{24,40},{28,44},{32,4... | collective-permute-start | bytes 4616 | tf_op jit(solution)/shard_map/while/body/eval_jaxpr/ppermute | solution.py:9
  56.7 8.5 %collective-permute-done = bf16[64,12]{1,0:T(8,128)(2,1)S(1)} collective-permute-done((bf16[64,12]{1,0:T(8,128)(2,1)S(1)}, bf16[64,12]{1,0:T(8,128)(2,1)S(1)}, u32[]{:S(2)}, u32[]{:S(2)}) %collective-permute-start) | collective-permute-done | bytes 1568 | tf_op jit(solution)/shard_map/while/body/eval_jaxpr/ppermute | solution.py:9
  67.6 5.7 %collective-permute-start = (bf16[64,12]{1,0:T(8,128)(2,1)S(1)}, bf16[64,12]{1,0:T(8,128)(2,1)S(1)}, u32[]{:S(2)}, u32[]{:S(2)}) collective-permute-start(bf16[64,12]{1,0:T(8,128)(2,1)S(1)} %get-tuple-element.235), channel_id=1, source_target_pairs={{0,16},{4,20},{8,24},{12,28},{16,32},{20,36},{24,40},{28,44},{32,4... | collective-permute-start | bytes 4616 | tf_op jit(solution)/shard_map/while/body/eval_jaxpr/ppermute | solution.py:9
  73.3 11.1 %collective-permute-done = bf16[64,12]{1,0:T(8,128)(2,1)S(1)} collective-permute-done((bf16[64,12]{1,0:T(8,128)(2,1)S(1)}, bf16[64,12]{1,0:T(8,128)(2,1)S(1)}, u32[]{:S(2)}, u32[]{:S(2)}) %collective-permute-start) | collective-permute-done | bytes 1568 | tf_op jit(solution)/shard_map/while/body/eval_jaxpr/ppermute | solution.py:9
  88.3 10.4 %collective-permute-done = bf16[64,12]{1,0:T(8,128)(2,1)S(1)} collective-permute-done((bf16[64,12]{1,0:T(8,128)(2,1)S(1)}, bf16[64,12]{1,0:T(8,128)(2,1)S(1)}, u32[]{:S(2)}, u32[]{:S(2)}) %collective-permute-start) | collective-permute-done | bytes 1568 | tf_op jit(solution)/shard_map/while/body/eval_jaxpr/ppermute | solution.py:9
  100.5 3.6 %collective-permute-start = (bf16[64,12]{1,0:T(8,128)(2,1)S(1)}, bf16[64,12]{1,0:T(8,128)(2,1)S(1)}, u32[]{:S(2)}, u32[]{:S(2)}) collective-permute-start(bf16[64,12]{1,0:T(8,128)(2,1)S(1)} %get-tuple-element.235), channel_id=1, source_target_pairs={{0,16},{4,20},{8,24},{12,28},{16,32},{20,36},{24,40},{28,44},{32,4... | collective-permute-start | bytes 4616 | tf_op jit(solution)/shard_map/while/body/eval_jaxpr/ppermute | solution.py:9
  104.1 8.2 %collective-permute-done = bf16[64,12]{1,0:T(8,128)(2,1)S(1)} collective-permute-done((bf16[64,12]{1,0:T(8,128)(2,1)S(1)}, bf16[64,12]{1,0:T(8,128)(2,1)S(1)}, u32[]{:S(2)}, u32[]{:S(2)}) %collective-permute-start) | collective-permute-done | bytes 1568 | tf_op jit(solution)/shard_map/while/body/eval_jaxpr/ppermute | solution.py:9
  114.1 4.6 %collective-permute-start = (bf16[64,12]{1,0:T(8,128)(2,1)S(1)}, bf16[64,12]{1,0:T(8,128)(2,1)S(1)}, u32[]{:S(2)}, u32[]{:S(2)}) collective-permute-start(bf16[64,12]{1,0:T(8,128)(2,1)S(1)} %get-tuple-element.235), channel_id=1, source_target_pairs={{0,16},{4,20},{8,24},{12,28},{16,32},{20,36},{24,40},{28,44},{32,4... | collective-permute-start | bytes 4616 | tf_op jit(solution)/shard_map/while/body/eval_jaxpr/ppermute | solution.py:9
  118.7 7.1 %collective-permute-done = bf16[64,12]{1,0:T(8,128)(2,1)S(1)} collective-permute-done((bf16[64,12]{1,0:T(8,128)(2,1)S(1)}, bf16[64,12]{1,0:T(8,128)(2,1)S(1)}, u32[]{:S(2)}, u32[]{:S(2)}) %collective-permute-start) | collective-permute-done | bytes 1568 | tf_op jit(solution)/shard_map/while/body/eval_jaxpr/ppermute | solution.py:9
  127.6 5.4 %collective-permute-start = (bf16[64,12]{1,0:T(8,128)(2,1)S(1)}, bf16[64,12]{1,0:T(8,128)(2,1)S(1)}, u32[]{:S(2)}, u32[]{:S(2)}) collective-permute-start(bf16[64,12]{1,0:T(8,128)(2,1)S(1)} %get-tuple-element.235), channel_id=1, source_target_pairs={{0,16},{4,20},{8,24},{12,28},{16,32},{20,36},{24,40},{28,44},{32,4... | collective-permute-start | bytes 4616 | tf_op jit(solution)/shard_map/while/body/eval_jaxpr/ppermute | solution.py:9
  132.9 6.3 %collective-permute-done = bf16[64,12]{1,0:T(8,128)(2,1)S(1)} collective-permute-done((bf16[64,12]{1,0:T(8,128)(2,1)S(1)}, bf16[64,12]{1,0:T(8,128)(2,1)S(1)}, u32[]{:S(2)}, u32[]{:S(2)}) %collective-permute-start) | collective-permute-done | bytes 1568 | tf_op jit(solution)/shard_map/while/body/eval_jaxpr/ppermute | solution.py:9
  141.2 6.4 %collective-permute-start = (bf16[64,12]{1,0:T(8,128)(2,1)S(1)}, bf16[64,12]{1,0:T(8,128)(2,1)S(1)}, u32[]{:S(2)}, u32[]{:S(2)}) collective-permute-start(bf16[64,12]{1,0:T(8,128)(2,1)S(1)} %get-tuple-element.235), channel_id=1, source_target_pairs={{0,16},{4,20},{8,24},{12,28},{16,32},{20,36},{24,40},{28,44},{32,4... | collective-permute-start | bytes 4616 | tf_op jit(solution)/shard_map/while/body/eval_jaxpr/ppermute | solution.py:9
  147.6 5.0 %collective-permute-done = bf16[64,12]{1,0:T(8,128)(2,1)S(1)} collective-permute-done((bf16[64,12]{1,0:T(8,128)(2,1)S(1)}, bf16[64,12]{1,0:T(8,128)(2,1)S(1)}, u32[]{:S(2)}, u32[]{:S(2)}) %collective-permute-start) | collective-permute-done | bytes 1568 | tf_op jit(solution)/shard_map/while/body/eval_jaxpr/ppermute | solution.py:9
  156.0 3.0 collective-permute-start
  159.0 7.0 %collective-permute-done = bf16[64,12]{1,0:T(8,128)(2,1)S(1)} collective-permute-done((bf16[64,12]{1,0:T(8,128)(2,1)S(1)}, bf16[64,12]{1,0:T(8,128)(2,1)S(1)}, u32[]{:S(2)}, u32[]{:S(2)}) %collective-permute-start) | collective-permute-done | bytes 1568 | tf_op jit(solution)/shard_map/while/body/eval_jaxpr/ppermute | solution.py:9
  170.4 10.0 %collective-permute-done = bf16[64,12]{1,0:T(8,128)(2,1)S(1)} collective-permute-done((bf16[64,12]{1,0:T(8,128)(2,1)S(1)}, bf16[64,12]{1,0:T(8,128)(2,1)S(1)}, u32[]{:S(2)}, u32[]{:S(2)}) %collective-permute-start) | collective-permute-done | bytes 1568 | tf_op jit(solution)/shard_map/while/body/eval_jaxpr/ppermute | solution.py:9
  183.6 12.2 %collective-permute-done = bf16[64,12]{1,0:T(8,128)(2,1)S(1)} collective-permute-done((bf16[64,12]{1,0:T(8,128)(2,1)S(1)}, bf16[64,12]{1,0:T(8,128)(2,1)S(1)}, u32[]{:S(2)}, u32[]{:S(2)}) %collective-permute-start) | collective-permute-done | bytes 1568 | tf_op jit(solution)/shard_map/while/body/eval_jaxpr/ppermute | solution.py:9
  197.7 13.2 %collective-permute-done = bf16[64,12]{1,0:T(8,128)(2,1)S(1)} collective-permute-done((bf16[64,12]{1,0:T(8,128)(2,1)S(1)}, bf16[64,12]{1,0:T(8,128)(2,1)S(1)}, u32[]{:S(2)}, u32[]{:S(2)}) %collective-permute-start) | collective-permute-done | bytes 1568 | tf_op jit(solution)/shard_map/while/body/eval_jaxpr/ppermute | solution.py:9
  212.9 14.1 %collective-permute-done = bf16[64,12]{1,0:T(8,128)(2,1)S(1)} collective-permute-done((bf16[64,12]{1,0:T(8,128)(2,1)S(1)}, bf16[64,12]{1,0:T(8,128)(2,1)S(1)}, u32[]{:S(2)}, u32[]{:S(2)}) %collective-permute-start) | collective-permute-done | bytes 1568 | tf_op jit(solution)/shard_map/while/body/eval_jaxpr/ppermute | solution.py:9
  228.9 12.3 %collective-permute-done = bf16[64,12]{1,0:T(8,128)(2,1)S(1)} collective-permute-done((bf16[64,12]{1,0:T(8,128)(2,1)S(1)}, bf16[64,12]{1,0:T(8,128)(2,1)S(1)}, u32[]{:S(2)}, u32[]{:S(2)}) %collective-permute-start) | collective-permute-done | bytes 1568 | tf_op jit(solution)/shard_map/while/body/eval_jaxpr/ppermute | solution.py:9
  243.7 11.0 %collective-permute-done = bf16[64,12]{1,0:T(8,128)(2,1)S(1)} collective-permute-done((bf16[64,12]{1,0:T(8,128)(2,1)S(1)}, bf16[64,12]{1,0:T(8,128)(2,1)S(1)}, u32[]{:S(2)}, u32[]{:S(2)}) %collective-permute-start) | collective-permute-done | bytes 1568 | tf_op jit(solution)/shard_map/while/body/eval_jaxpr/ppermute | solution.py:9
  257.9 10.3 %collective-permute-done = bf16[64,12]{1,0:T(8,128)(2,1)S(1)} collective-permute-done((bf16[64,12]{1,0:T(8,128)(2,1)S(1)}, bf16[64,12]{1,0:T(8,128)(2,1)S(1)}, u32[]{:S(2)}, u32[]{:S(2)}) %collective-permute-start) | collective-permute-done | bytes 1568 | tf_op jit(solution)/shard_map/while/body/eval_jaxpr/ppermute | solution.py:9
  269.9 45.7 %all-gather = f32[256,256]{1,0:T(8,128)S(1)} all-gather(f32[64,256]{1,0:T(8,128)S(1)} %get-tuple-element.160), channel_id=2, replica_groups=mesh['blk'=64,'team'=4] {'team'}, dimensions={0}, use_global_device_ids=true | all-gather | bytes 327680 | tf_op jit(solution)/shard_map/all_gather | solution.py:66
  (115 shorter events, 40.8 us)
Async XLA Ops:
  10.4 20.6 %collective-permute-start.2 = (bf16[64,1536]{1,0:T(8,128)(2,1)S(1)}, bf16[64,1536]{1,0:T(8,128)(2,1)S(1)}, u32[]{:S(2)}, u32[]{:S(2)}) collective-permute-start(bf16[64,1536]{1,0:T(8,128)(2,1)S(1)} %all_gather.12), channel_id=1, source_target_pairs={{0,4},{4,8},{8,12},{12,16},{16,20},{20,24},{24,28},{28,32},{32,36}... | collective-permute-start | bytes 589832 | tf_op jit(solution)/shard_map/ppermute | solution.py:9
  10.4 39.0 %collective-permute-start.3 = (bf16[64,1536]{1,0:T(8,128)(2,1)S(1)}, bf16[64,1536]{1,0:T(8,128)(2,1)S(1)}, u32[]{:S(2)}, u32[]{:S(2)}) collective-permute-start(bf16[64,1536]{1,0:T(8,128)(2,1)S(1)} %all_gather.12), channel_id=1, source_target_pairs={{0,8},{4,12},{8,16},{12,20},{16,24},{20,28},{24,32},{28,36},{32,40... | collective-permute-start | bytes 589832 | tf_op jit(solution)/shard_map/ppermute | solution.py:9
  23.5 25.6 %collective-permute-start.6 = (bf16[64,12]{0,1:T(8,128)(2,1)S(1)}, bf16[64,12]{0,1:T(8,128)(2,1)S(1)}, u32[]{:S(2)}, u32[]{:S(2)}) collective-permute-start(bf16[64,12]{0,1:T(8,128)(2,1)S(1)} %bitcast.52), channel_id=1, source_target_pairs={{0,8},{4,12},{8,16},{12,20},{16,24},{20,28},{24,32},{28,36},{32,40... | collective-permute-start | bytes 4616 | tf_op jit(solution)/shard_map/ppermute | solution.py:9
  31.0 18.1 %collective-permute-start.7 = (bf16[64,12]{0,1:T(8,128)(2,1)S(1)}, bf16[64,12]{0,1:T(8,128)(2,1)S(1)}, u32[]{:S(2)}, u32[]{:S(2)}) collective-permute-start(bf16[64,12]{0,1:T(8,128)(2,1)S(1)} %collective-permute-done.5), channel_id=1, source_target_pairs={{0,8},{4,12},{8,16},{12,20},{16,24},{20,28},{24,32},{28,36},{32,40... | collective-permute-start | bytes 4616 | tf_op jit(solution)/shard_map/ppermute | solution.py:9
  31.0 18.4 %collective-permute-start.4 = (bf16[64,1536]{1,0:T(8,128)(2,1)S(1)}, bf16[64,1536]{1,0:T(8,128)(2,1)S(1)}, u32[]{:S(2)}, u32[]{:S(2)}) collective-permute-start(bf16[64,1536]{1,0:T(8,128)(2,1)S(1)} %collective-permute-done.2), channel_id=1, source_target_pairs={{0,8},{4,12},{8,16},{12,20},{16,24},{20,28},{24,32},{28,36},{32,40... | collective-permute-start | bytes 589832 | tf_op jit(solution)/shard_map/ppermute | solution.py:9
  50.3 14.9 %collective-permute-start.1 = (bf16[64,1536]{1,0:T(8,128)(2,1)S(1)}, bf16[64,1536]{1,0:T(8,128)(2,1)S(1)}, u32[]{:S(2)}, u32[]{:S(2)}) collective-permute-start(bf16[64,1536]{1,0:T(8,128)(2,1)S(1)} %get-tuple-element.234), channel_id=1, source_target_pairs={{0,16},{4,20},{8,24},{12,28},{16,32},{20,36},{24,40},{28,44},{32,4... | collective-permute-start | bytes 589832 | tf_op jit(solution)/shard_map/while/body/eval_jaxpr/ppermute | solution.py:9
  52.9 12.3 %collective-permute-start = (bf16[64,12]{1,0:T(8,128)(2,1)S(1)}, bf16[64,12]{1,0:T(8,128)(2,1)S(1)}, u32[]{:S(2)}, u32[]{:S(2)}) collective-permute-start(bf16[64,12]{1,0:T(8,128)(2,1)S(1)} %get-tuple-element.235), channel_id=1, source_target_pairs={{0,16},{4,20},{8,24},{12,28},{16,32},{20,36},{24,40},{28,44},{32,4... | collective-permute-start | bytes 4616 | tf_op jit(solution)/shard_map/while/body/eval_jaxpr/ppermute | solution.py:9
  66.9 17.6 %collective-permute-start.1 = (bf16[64,1536]{1,0:T(8,128)(2,1)S(1)}, bf16[64,1536]{1,0:T(8,128)(2,1)S(1)}, u32[]{:S(2)}, u32[]{:S(2)}) collective-permute-start(bf16[64,1536]{1,0:T(8,128)(2,1)S(1)} %get-tuple-element.234), channel_id=1, source_target_pairs={{0,16},{4,20},{8,24},{12,28},{16,32},{20,36},{24,40},{28,44},{32,4... | collective-permute-start | bytes 589832 | tf_op jit(solution)/shard_map/while/body/eval_jaxpr/ppermute | solution.py:9
  67.6 16.8 %collective-permute-start = (bf16[64,12]{1,0:T(8,128)(2,1)S(1)}, bf16[64,12]{1,0:T(8,128)(2,1)S(1)}, u32[]{:S(2)}, u32[]{:S(2)}) collective-permute-start(bf16[64,12]{1,0:T(8,128)(2,1)S(1)} %get-tuple-element.235), channel_id=1, source_target_pairs={{0,16},{4,20},{8,24},{12,28},{16,32},{20,36},{24,40},{28,44},{32,4... | collective-permute-start | bytes 4616 | tf_op jit(solution)/shard_map/while/body/eval_jaxpr/ppermute | solution.py:9
  86.2 12.5 %collective-permute-start.1 = (bf16[64,1536]{1,0:T(8,128)(2,1)S(1)}, bf16[64,1536]{1,0:T(8,128)(2,1)S(1)}, u32[]{:S(2)}, u32[]{:S(2)}) collective-permute-start(bf16[64,1536]{1,0:T(8,128)(2,1)S(1)} %get-tuple-element.234), channel_id=1, source_target_pairs={{0,16},{4,20},{8,24},{12,28},{16,32},{20,36},{24,40},{28,44},{32,4... | collective-permute-start | bytes 589832 | tf_op jit(solution)/shard_map/while/body/eval_jaxpr/ppermute | solution.py:9
  86.3 12.4 %collective-permute-start = (bf16[64,12]{1,0:T(8,128)(2,1)S(1)}, bf16[64,12]{1,0:T(8,128)(2,1)S(1)}, u32[]{:S(2)}, u32[]{:S(2)}) collective-permute-start(bf16[64,12]{1,0:T(8,128)(2,1)S(1)} %get-tuple-element.235), channel_id=1, source_target_pairs={{0,16},{4,20},{8,24},{12,28},{16,32},{20,36},{24,40},{28,44},{32,4... | collective-permute-start | bytes 4616 | tf_op jit(solution)/shard_map/while/body/eval_jaxpr/ppermute | solution.py:9
  100.4 11.9 %collective-permute-start.1 = (bf16[64,1536]{1,0:T(8,128)(2,1)S(1)}, bf16[64,1536]{1,0:T(8,128)(2,1)S(1)}, u32[]{:S(2)}, u32[]{:S(2)}) collective-permute-start(bf16[64,1536]{1,0:T(8,128)(2,1)S(1)} %get-tuple-element.234), channel_id=1, source_target_pairs={{0,16},{4,20},{8,24},{12,28},{16,32},{20,36},{24,40},{28,44},{32,4... | collective-permute-start | bytes 589832 | tf_op jit(solution)/shard_map/while/body/eval_jaxpr/ppermute | solution.py:9
  100.5 11.8 %collective-permute-start = (bf16[64,12]{1,0:T(8,128)(2,1)S(1)}, bf16[64,12]{1,0:T(8,128)(2,1)S(1)}, u32[]{:S(2)}, u32[]{:S(2)}) collective-permute-start(bf16[64,12]{1,0:T(8,128)(2,1)S(1)} %get-tuple-element.235), channel_id=1, source_target_pairs={{0,16},{4,20},{8,24},{12,28},{16,32},{20,36},{24,40},{28,44},{32,4... | collective-permute-start | bytes 4616 | tf_op jit(solution)/shard_map/while/body/eval_jaxpr/ppermute | solution.py:9
  114.0 11.8 %collective-permute-start.1 = (bf16[64,1536]{1,0:T(8,128)(2,1)S(1)}, bf16[64,1536]{1,0:T(8,128)(2,1)S(1)}, u32[]{:S(2)}, u32[]{:S(2)}) collective-permute-start(bf16[64,1536]{1,0:T(8,128)(2,1)S(1)} %get-tuple-element.234), channel_id=1, source_target_pairs={{0,16},{4,20},{8,24},{12,28},{16,32},{20,36},{24,40},{28,44},{32,4... | collective-permute-start | bytes 589832 | tf_op jit(solution)/shard_map/while/body/eval_jaxpr/ppermute | solution.py:9
  114.1 11.7 %collective-permute-start = (bf16[64,12]{1,0:T(8,128)(2,1)S(1)}, bf16[64,12]{1,0:T(8,128)(2,1)S(1)}, u32[]{:S(2)}, u32[]{:S(2)}) collective-permute-start(bf16[64,12]{1,0:T(8,128)(2,1)S(1)} %get-tuple-element.235), channel_id=1, source_target_pairs={{0,16},{4,20},{8,24},{12,28},{16,32},{20,36},{24,40},{28,44},{32,4... | collective-permute-start | bytes 4616 | tf_op jit(solution)/shard_map/while/body/eval_jaxpr/ppermute | solution.py:9
  127.5 11.7 %collective-permute-start.1 = (bf16[64,1536]{1,0:T(8,128)(2,1)S(1)}, bf16[64,1536]{1,0:T(8,128)(2,1)S(1)}, u32[]{:S(2)}, u32[]{:S(2)}) collective-permute-start(bf16[64,1536]{1,0:T(8,128)(2,1)S(1)} %get-tuple-element.234), channel_id=1, source_target_pairs={{0,16},{4,20},{8,24},{12,28},{16,32},{20,36},{24,40},{28,44},{32,4... | collective-permute-start | bytes 589832 | tf_op jit(solution)/shard_map/while/body/eval_jaxpr/ppermute | solution.py:9
  141.0 11.7 %collective-permute-start.1 = (bf16[64,1536]{1,0:T(8,128)(2,1)S(1)}, bf16[64,1536]{1,0:T(8,128)(2,1)S(1)}, u32[]{:S(2)}, u32[]{:S(2)}) collective-permute-start(bf16[64,1536]{1,0:T(8,128)(2,1)S(1)} %get-tuple-element.234), channel_id=1, source_target_pairs={{0,16},{4,20},{8,24},{12,28},{16,32},{20,36},{24,40},{28,44},{32,4... | collective-permute-start | bytes 589832 | tf_op jit(solution)/shard_map/while/body/eval_jaxpr/ppermute | solution.py:9
  154.4 11.7 %collective-permute-start.1 = (bf16[64,1536]{1,0:T(8,128)(2,1)S(1)}, bf16[64,1536]{1,0:T(8,128)(2,1)S(1)}, u32[]{:S(2)}, u32[]{:S(2)}) collective-permute-start(bf16[64,1536]{1,0:T(8,128)(2,1)S(1)} %get-tuple-element.234), channel_id=1, source_target_pairs={{0,16},{4,20},{8,24},{12,28},{16,32},{20,36},{24,40},{28,44},{32,4... | collective-permute-start | bytes 589832 | tf_op jit(solution)/shard_map/while/body/eval_jaxpr/ppermute | solution.py:9
  167.8 12.6 %collective-permute-start.1 = (bf16[64,1536]{1,0:T(8,128)(2,1)S(1)}, bf16[64,1536]{1,0:T(8,128)(2,1)S(1)}, u32[]{:S(2)}, u32[]{:S(2)}) collective-permute-start(bf16[64,1536]{1,0:T(8,128)(2,1)S(1)} %get-tuple-element.234), channel_id=1, source_target_pairs={{0,16},{4,20},{8,24},{12,28},{16,32},{20,36},{24,40},{28,44},{32,4... | collective-permute-start | bytes 589832 | tf_op jit(solution)/shard_map/while/body/eval_jaxpr/ppermute | solution.py:9
  168.5 11.8 %collective-permute-start = (bf16[64,12]{1,0:T(8,128)(2,1)S(1)}, bf16[64,12]{1,0:T(8,128)(2,1)S(1)}, u32[]{:S(2)}, u32[]{:S(2)}) collective-permute-start(bf16[64,12]{1,0:T(8,128)(2,1)S(1)} %get-tuple-element.235), channel_id=1, source_target_pairs={{0,16},{4,20},{8,24},{12,28},{16,32},{20,36},{24,40},{28,44},{32,4... | collective-permute-start | bytes 4616 | tf_op jit(solution)/shard_map/while/body/eval_jaxpr/ppermute | solution.py:9
  182.1 13.7 %collective-permute-start.1 = (bf16[64,1536]{1,0:T(8,128)(2,1)S(1)}, bf16[64,1536]{1,0:T(8,128)(2,1)S(1)}, u32[]{:S(2)}, u32[]{:S(2)}) collective-permute-start(bf16[64,1536]{1,0:T(8,128)(2,1)S(1)} %get-tuple-element.234), channel_id=1, source_target_pairs={{0,16},{4,20},{8,24},{12,28},{16,32},{20,36},{24,40},{28,44},{32,4... | collective-permute-start | bytes 589832 | tf_op jit(solution)/shard_map/while/body/eval_jaxpr/ppermute | solution.py:9
  182.2 13.6 %collective-permute-start = (bf16[64,12]{1,0:T(8,128)(2,1)S(1)}, bf16[64,12]{1,0:T(8,128)(2,1)S(1)}, u32[]{:S(2)}, u32[]{:S(2)}) collective-permute-start(bf16[64,12]{1,0:T(8,128)(2,1)S(1)} %get-tuple-element.235), channel_id=1, source_target_pairs={{0,16},{4,20},{8,24},{12,28},{16,32},{20,36},{24,40},{28,44},{32,4... | collective-permute-start | bytes 4616 | tf_op jit(solution)/shard_map/while/body/eval_jaxpr/ppermute | solution.py:9
  197.5 13.4 %collective-permute-start.1 = (bf16[64,1536]{1,0:T(8,128)(2,1)S(1)}, bf16[64,1536]{1,0:T(8,128)(2,1)S(1)}, u32[]{:S(2)}, u32[]{:S(2)}) collective-permute-start(bf16[64,1536]{1,0:T(8,128)(2,1)S(1)} %get-tuple-element.234), channel_id=1, source_target_pairs={{0,16},{4,20},{8,24},{12,28},{16,32},{20,36},{24,40},{28,44},{32,4... | collective-permute-start | bytes 589832 | tf_op jit(solution)/shard_map/while/body/eval_jaxpr/ppermute | solution.py:9
  197.6 13.3 %collective-permute-start = (bf16[64,12]{1,0:T(8,128)(2,1)S(1)}, bf16[64,12]{1,0:T(8,128)(2,1)S(1)}, u32[]{:S(2)}, u32[]{:S(2)}) collective-permute-start(bf16[64,12]{1,0:T(8,128)(2,1)S(1)} %get-tuple-element.235), channel_id=1, source_target_pairs={{0,16},{4,20},{8,24},{12,28},{16,32},{20,36},{24,40},{28,44},{32,4... | collective-permute-start | bytes 4616 | tf_op jit(solution)/shard_map/while/body/eval_jaxpr/ppermute | solution.py:9
  212.7 14.3 %collective-permute-start.1 = (bf16[64,1536]{1,0:T(8,128)(2,1)S(1)}, bf16[64,1536]{1,0:T(8,128)(2,1)S(1)}, u32[]{:S(2)}, u32[]{:S(2)}) collective-permute-start(bf16[64,1536]{1,0:T(8,128)(2,1)S(1)} %get-tuple-element.234), channel_id=1, source_target_pairs={{0,16},{4,20},{8,24},{12,28},{16,32},{20,36},{24,40},{28,44},{32,4... | collective-permute-start | bytes 589832 | tf_op jit(solution)/shard_map/while/body/eval_jaxpr/ppermute | solution.py:9
  212.8 14.2 %collective-permute-start = (bf16[64,12]{1,0:T(8,128)(2,1)S(1)}, bf16[64,12]{1,0:T(8,128)(2,1)S(1)}, u32[]{:S(2)}, u32[]{:S(2)}) collective-permute-start(bf16[64,12]{1,0:T(8,128)(2,1)S(1)} %get-tuple-element.235), channel_id=1, source_target_pairs={{0,16},{4,20},{8,24},{12,28},{16,32},{20,36},{24,40},{28,44},{32,4... | collective-permute-start | bytes 4616 | tf_op jit(solution)/shard_map/while/body/eval_jaxpr/ppermute | solution.py:9
  228.7 12.5 %collective-permute-start.1 = (bf16[64,1536]{1,0:T(8,128)(2,1)S(1)}, bf16[64,1536]{1,0:T(8,128)(2,1)S(1)}, u32[]{:S(2)}, u32[]{:S(2)}) collective-permute-start(bf16[64,1536]{1,0:T(8,128)(2,1)S(1)} %get-tuple-element.234), channel_id=1, source_target_pairs={{0,16},{4,20},{8,24},{12,28},{16,32},{20,36},{24,40},{28,44},{32,4... | collective-permute-start | bytes 589832 | tf_op jit(solution)/shard_map/while/body/eval_jaxpr/ppermute | solution.py:9
  228.8 12.4 %collective-permute-start = (bf16[64,12]{1,0:T(8,128)(2,1)S(1)}, bf16[64,12]{1,0:T(8,128)(2,1)S(1)}, u32[]{:S(2)}, u32[]{:S(2)}) collective-permute-start(bf16[64,12]{1,0:T(8,128)(2,1)S(1)} %get-tuple-element.235), channel_id=1, source_target_pairs={{0,16},{4,20},{8,24},{12,28},{16,32},{20,36},{24,40},{28,44},{32,4... | collective-permute-start | bytes 4616 | tf_op jit(solution)/shard_map/while/body/eval_jaxpr/ppermute | solution.py:9
  242.9 11.8 %collective-permute-start.1 = (bf16[64,1536]{1,0:T(8,128)(2,1)S(1)}, bf16[64,1536]{1,0:T(8,128)(2,1)S(1)}, u32[]{:S(2)}, u32[]{:S(2)}) collective-permute-start(bf16[64,1536]{1,0:T(8,128)(2,1)S(1)} %get-tuple-element.234), channel_id=1, source_target_pairs={{0,16},{4,20},{8,24},{12,28},{16,32},{20,36},{24,40},{28,44},{32,4... | collective-permute-start | bytes 589832 | tf_op jit(solution)/shard_map/while/body/eval_jaxpr/ppermute | solution.py:9
  243.0 11.7 %collective-permute-start = (bf16[64,12]{1,0:T(8,128)(2,1)S(1)}, bf16[64,12]{1,0:T(8,128)(2,1)S(1)}, u32[]{:S(2)}, u32[]{:S(2)}) collective-permute-start(bf16[64,12]{1,0:T(8,128)(2,1)S(1)} %get-tuple-element.235), channel_id=1, source_target_pairs={{0,16},{4,20},{8,24},{12,28},{16,32},{20,36},{24,40},{28,44},{32,4... | collective-permute-start | bytes 4616 | tf_op jit(solution)/shard_map/while/body/eval_jaxpr/ppermute | solution.py:9
  256.4 11.8 %collective-permute-start.1 = (bf16[64,1536]{1,0:T(8,128)(2,1)S(1)}, bf16[64,1536]{1,0:T(8,128)(2,1)S(1)}, u32[]{:S(2)}, u32[]{:S(2)}) collective-permute-start(bf16[64,1536]{1,0:T(8,128)(2,1)S(1)} %get-tuple-element.234), channel_id=1, source_target_pairs={{0,16},{4,20},{8,24},{12,28},{16,32},{20,36},{24,40},{28,44},{32,4... | collective-permute-start | bytes 589832 | tf_op jit(solution)/shard_map/while/body/eval_jaxpr/ppermute | solution.py:9
  256.5 11.7 %collective-permute-start = (bf16[64,12]{1,0:T(8,128)(2,1)S(1)}, bf16[64,12]{1,0:T(8,128)(2,1)S(1)}, u32[]{:S(2)}, u32[]{:S(2)}) collective-permute-start(bf16[64,12]{1,0:T(8,128)(2,1)S(1)} %get-tuple-element.235), channel_id=1, source_target_pairs={{0,16},{4,20},{8,24},{12,28},{16,32},{20,36},{24,40},{28,44},{32,4... | collective-permute-start | bytes 4616 | tf_op jit(solution)/shard_map/while/body/eval_jaxpr/ppermute | solution.py:9
  (4 other events, 43.5 us)
